TPU v7x, 32 devices: a whole 2x2x4 slice. The times are simulated.
32 devices in a mesh: ctx: 16 (over z, y, core), head: 2 (over x).
Axes of the slice: x: 2, y: 2, z: 4, core: 2. Of those that a mesh axis runs over, the one named last changes fastest.
Arguments:
- queries: bfloat16 [2048, 1536], P('ctx', 'head'), may hold values from -45 to 45
- key_rows: bfloat16 [2048, 256], P('ctx', 'head'), may hold values from -5 to 5
- value_rows: bfloat16 [2048, 256], P('ctx', 'head'), may hold values from -18 to 18
- cotangent: bfloat16 [2048, 1536], P('ctx', 'head'), may hold values from -6 to 6
- trace_ids: int32 [2048], P('ctx'), may hold values from 0 to 15, never falling along the last dimension, each value on 1 to 512 neighbouring positions
- correct: int32 [16], replicated, may hold values from 0 to 16, as said below
- group_size: int32 [16], replicated, may hold values from 4 to 16
Outputs:
- log_totals: float32 [2048, 12], P('ctx', 'head')
- grad_queries: float32 [2048, 1536], P('ctx', 'head')
- grad_keys: bfloat16 [2048, 256], P('ctx', 'head')
- grad_values: bfloat16 [2048, 256], P('ctx', 'head')
Inputs may be any that keep to these rules, and one draw needn't show every extreme that they name: correct[g] is at most group_size[g].
All inputs are finite; a program needn't handle non-finite values.
Results may differ from a plain program's by a relative error of at most 0.0054.
Values may be sent and summed in bfloat16 or wider, within the bound.
No kernel may reach another device: no remote copies, remote signals or barrier semaphores. Data moves between devices by JAX's collectives and lax.ppermute only.
A program may use at most 64 MiB of HBM per device.

v0:
```python
import math
import jax
import jax.numpy as jnp
from jax import lax
from jax.sharding import PartitionSpec as P

PASSK = 4


def pass_rate(correct, group_size):
    counts = group_size.astype(jnp.float32)
    hit_counts = correct.astype(jnp.float32)
    product = jnp.ones_like(counts)
    for offset in range(PASSK):
        product = product * (counts - hit_counts - offset) / (counts - offset)
    return 1.0 - product


def body(queries, key_rows, value_rows, cotangent, trace_ids, correct, group_size):
    tok_rows = queries.shape[0]
    half_rows = tok_rows // 2
    row_width = queries.shape[1]
    head_dim = key_rows.shape[1]
    head_count = row_width // head_dim
    ctx_count = lax.axis_size("ctx")
    my_index = lax.axis_index("ctx")
    length = tok_rows * ctx_count
    score_scale = 1.0 / math.sqrt(head_dim)
    pass_rates = pass_rate(correct, group_size)
    traces = jnp.arange(pass_rates.shape[0], dtype=jnp.int32)
    weights = jnp.sum(
        jnp.where(trace_ids[:, None] == traces[None, :], pass_rates[None, :], 0.0), axis=1
    )
    out_grads = (weights[:, None] * cotangent.astype(jnp.float32)).astype(jnp.bfloat16)
    first_base = my_index * tok_rows
    second_base = first_base + half_rows
    local_pos = jnp.arange(half_rows, dtype=jnp.int32)
    positions = jnp.concatenate([first_base + local_pos, second_base + local_pos], 0)
    last_first = first_base + half_rows - 1
    last_second = second_base + half_rows - 1
    query_all = queries.reshape(tok_rows, head_count, head_dim)
    grad_all = out_grads.reshape(tok_rows, head_count, head_dim)

    def run_block(running, key_block, value_block, key_start, block_fn):
        need_first = (key_start <= last_first).astype(jnp.int32)
        need_second = (key_start <= last_second).astype(jnp.int32)
        branch_index = need_first + 2 * need_second

        def skip_block(values_in):
            return values_in

        def first_only(values_in):
            return block_fn((0, half_rows), values_in, key_block, value_block, key_start)

        def second_only(values_in):
            return block_fn((half_rows, tok_rows), values_in, key_block, value_block, key_start)

        def both_halves(values_in):
            return block_fn((0, tok_rows), values_in, key_block, value_block, key_start)

        return lax.switch(branch_index, [skip_block, first_only, second_only, both_halves], running)

    def forward_block(row_span, running, key_block, value_block, key_start):
        row_begin, row_end = row_span
        row_peak, row_total, weighted = running
        query_part = query_all[row_begin:row_end]
        grad_part = grad_all[row_begin:row_end]
        query_pos = positions[row_begin:row_end]
        scores = (
            jnp.einsum("tqd,kd->tqk", query_part, key_block, preferred_element_type=jnp.float32)
            * score_scale
        )
        key_pos = key_start + jnp.arange(key_block.shape[0], dtype=jnp.int32)
        visible = key_pos[None, None, :] <= query_pos[:, None, None]
        block_peak = jnp.max(jnp.where(visible, scores, -1e30), axis=2)
        old_peak = row_peak[row_begin:row_end]
        new_peak = jnp.maximum(old_peak, block_peak)
        exp_terms = jnp.where(visible, jnp.exp(scores - new_peak[:, :, None]), 0.0)
        grad_probs = jnp.einsum(
            "tqd,kd->tqk", grad_part, value_block, preferred_element_type=jnp.float32
        )
        shrink = jnp.exp(old_peak - new_peak)
        new_total = row_total[row_begin:row_end] * shrink + jnp.sum(exp_terms, axis=2)
        new_weighted = weighted[row_begin:row_end] * shrink + jnp.sum(
            exp_terms * grad_probs, axis=2
        )
        return (
            row_peak.at[row_begin:row_end].set(new_peak),
            row_total.at[row_begin:row_end].set(new_total),
            weighted.at[row_begin:row_end].set(new_weighted),
        )

    row_peak = jnp.full((tok_rows, head_count), -1e30, jnp.float32)
    row_total = jnp.zeros((tok_rows, head_count), jnp.float32)
    weighted = jnp.zeros((tok_rows, head_count), jnp.float32)
    key_piece = lax.all_gather(key_rows, "ctx", axis=0, tiled=True)
    value_piece = lax.all_gather(value_rows, "ctx", axis=0, tiled=True)
    piece_rows = key_piece.shape[0]
    block_rows = math.gcd(piece_rows, 512)

    def forward_step(step_index, statistics):
        offset = step_index * block_rows
        key_block = lax.dynamic_slice_in_dim(key_piece, offset, block_rows, 0)
        value_block = lax.dynamic_slice_in_dim(value_piece, offset, block_rows, 0)
        return run_block(statistics, key_block, value_block, offset, forward_block)

    statistics = lax.fori_loop(
        0, piece_rows // block_rows, forward_step, (row_peak, row_total, weighted)
    )
    folded = statistics + (key_piece, value_piece)
    row_peak, row_total, weighted, key_store, value_store = folded
    log_totals = row_peak + jnp.log(row_total)
    delta_rows = weighted / row_total

    def backward_block(row_span, running, key_block, value_block, key_start):
        row_begin, row_end = row_span
        grad_query, zero_block = running
        query_part = query_all[row_begin:row_end]
        grad_part = grad_all[row_begin:row_end]
        query_pos = positions[row_begin:row_end]
        scores = (
            jnp.einsum("tqd,kd->tqk", query_part, key_block, preferred_element_type=jnp.float32)
            * score_scale
        )
        key_pos = key_start + jnp.arange(key_block.shape[0], dtype=jnp.int32)
        visible = key_pos[None, None, :] <= query_pos[:, None, None]
        probabilities = jnp.where(
            visible, jnp.exp(scores - log_totals[row_begin:row_end][:, :, None]), 0.0
        )
        prob_bf16 = probabilities.astype(jnp.bfloat16)
        grad_probs = jnp.einsum(
            "tqd,kd->tqk", grad_part, value_block, preferred_element_type=jnp.float32
        )
        grad_scores = (
            probabilities * (grad_probs - delta_rows[row_begin:row_end][:, :, None])
        ).astype(jnp.bfloat16)
        query_add = (
            jnp.einsum("tqk,kd->tqd", grad_scores, key_block, preferred_element_type=jnp.float32)
            * score_scale
        )
        key_add = (
            jnp.einsum("tqk,tqd->kd", grad_scores, query_part, preferred_element_type=jnp.float32)
            * score_scale
        )
        value_add = jnp.einsum(
            "tqk,tqd->kd", prob_bf16, grad_part, preferred_element_type=jnp.float32
        )
        return (
            grad_query.at[row_begin:row_end].add(query_add),
            jnp.concatenate([key_add, value_add], 1),
        )

    query_zero = jnp.zeros((tok_rows, head_count, head_dim), jnp.float32)
    key_block_rows = math.gcd(length, 512)

    def backward_step(step_index, running):
        grad_query, partial_sums = running
        key_start = step_index * key_block_rows
        key_block = lax.dynamic_slice_in_dim(key_store, key_start, key_block_rows, 0)
        value_block = lax.dynamic_slice_in_dim(value_store, key_start, key_block_rows, 0)
        zero_block = jnp.zeros((key_block_rows, 2 * head_dim), jnp.float32)
        grad_query, block_sums = run_block(
            (grad_query, zero_block), key_block, value_block, key_start, backward_block
        )
        partial_sums = lax.dynamic_update_slice_in_dim(partial_sums, block_sums, key_start, 0)
        return (grad_query, partial_sums)

    grad_query, partial_sums = lax.fori_loop(
        0,
        length // key_block_rows,
        backward_step,
        (query_zero, jnp.zeros((length, 2 * head_dim), jnp.float32)),
    )
    reduced = jnp.sum(
        lax.all_to_all(
            partial_sums.reshape(ctx_count, tok_rows, 2 * head_dim),
            "ctx",
            split_axis=0,
            concat_axis=0,
            tiled=True,
        ),
        axis=0,
    )
    grad_keys = reduced[:, :head_dim].astype(jnp.bfloat16)
    grad_values = reduced[:, head_dim:].astype(jnp.bfloat16)
    query_grads = grad_query.reshape(tok_rows, row_width)
    return (log_totals, query_grads, grad_keys, grad_values)


def solution(mesh):
    return jax.shard_map(
        body,
        mesh=mesh,
        in_specs=(
            P("ctx", "head"),
            P("ctx", "head"),
            P("ctx", "head"),
            P("ctx", "head"),
            P("ctx"),
            P(),
            P(),
        ),
        out_specs=(P("ctx", "head"), P("ctx", "head"), P("ctx", "head"), P("ctx", "head")),
        check_vma=False,
    )
```

profile of v0, /device:TPU:13, one launch (start us, length us, event | category | flops | bytes accessed | tf_op | source)
XLA Modules:
  0.0 124.0 jit_solution(4631487437105801853)
XLA Ops:
  0.6 0.0 copy-start.1
  0.6 0.0 copy-start.2
  0.7 0.7 fusion.61
  1.4 0.7 select_reduce_fusion.3
  2.1 1.0 multiply_convert_fusion.1
  3.1 0.2 copy.73
  3.3 0.2 copy.75
  3.5 1.1 copy.72
  4.6 0.2 copy.74
  4.8 0.0 copy-done.1
  4.8 17.1 %all_gather.6 = bf16[2048,128]{1,0:T(8,128)(2,1)S(1)} all-gather(bf16[128,128]{1,0:T(8,128)(2,1)S(1)} %copy-done.1), channel_id=1, replica_groups=mesh['ctx'=16,'head'=2] {'ctx'}, dimensions={0}, use_global_device_ids=true | all-gather | bytes 557056 | tf_op jit(solution)/shard_map/all_gather | solution.py:96
  21.9 0.0 copy-done.2
  21.9 22.8 %all_gather.7 = bf16[2048,128]{1,0:T(8,128)(2,1)S(1)} all-gather(bf16[128,128]{1,0:T(8,128)(2,1)S(1)} %copy-done.2), channel_id=1, replica_groups=mesh['ctx'=16,'head'=2] {'ctx'}, dimensions={0}, use_global_device_ids=true | all-gather | bytes 557056 | tf_op jit(solution)/shard_map/all_gather | solution.py:97
  44.7 0.1 pad_add_fusion
  44.8 3.9 %while.53 = (s32[]{:T(128)}, f32[128,6]{0,1:T(8,128)S(1)}, f32[128,6]{0,1:T(8,128)S(1)}, f32[128,6]{0,1:T(8,128)S(1)}, s32[]{:T(128)}, /*index=5*/s32[]{:T(128)}...) while((s32[]{:T(128)}, f32[128,6]{0,1:T(8,128)S(1)}, ...), condition=%wide.region_15.0_spmd.clone, body=%wide.region_1.15_spmd.clone.sunk | while | flops 205327120 | bytes 6221379 | solution.py:107
  44.8 1.7 %conditional.6 = ((f32[128,6]{0,1:T(8,128)S(1)}, f32[128,6]{0,1:T(8,128)S(1)}, f32[128,6]{0,1:T(8,128)S(1)})) conditional(s32[]{:T(128)} %clamp.18, (f32[128,6]{0,1:T(8,128)S(1)}, f32[128,6]{0,1:T(8,128)S(1)}, f32[128,6]{0,1:T(8,128)S(1)}) %tuple.202, (f32[128,6]{0,1:T(8,128)S(1)}, s32[]{:T(128)}, s32[]{:T(128)}, ...), branch_computations={%region_2.2_spmd, %region_3.6_spmd, %region_7.10_spmd, %region_11.... | conditional | flops 205327104 | bytes 5696036 | solution.py:61
  44.9 0.1 broadcast_compare_fusion.2
  45.0 0.5 select_reduce_fusion.2
  45.4 0.6 multiply_reduce_fusion
  46.0 0.5 fusion.20
  46.6 1.7 %conditional.6 = ((f32[128,6]{0,1:T(8,128)S(1)}, f32[128,6]{0,1:T(8,128)S(1)}, f32[128,6]{0,1:T(8,128)S(1)})) conditional(s32[]{:T(128)} %clamp.18, (f32[128,6]{0,1:T(8,128)S(1)}, f32[128,6]{0,1:T(8,128)S(1)}, f32[128,6]{0,1:T(8,128)S(1)}) %tuple.202, (f32[128,6]{0,1:T(8,128)S(1)}, s32[]{:T(128)}, s32[]{:T(128)}, ...), branch_computations={%region_2.2_spmd, %region_3.6_spmd, %region_7.10_spmd, %region_11.... | conditional | flops 205327104 | bytes 5696036 | solution.py:61
  46.7 0.1 broadcast_compare_fusion.2
  46.8 0.5 select_reduce_fusion.2
  47.3 0.6 multiply_reduce_fusion
  47.8 0.5 fusion.20
  48.7 1.5 %broadcast_in_dim.124.clone = f32[2048,256]{1,0:T(8,128)} broadcast(f32[]{:T(128)} %constant.488.clone.1), dimensions={} | broadcast | bytes 2097156 | tf_op jit(solution)/shard_map/broadcast_in_dim | solution.py:172
  50.2 8.7 %while.54 = (s32[]{:T(128)}, f32[128,6,128]{2,0,1:T(8,128)S(1)}, f32[2048,256]{1,0:T(8,128)}, s32[]{:T(128)}, s32[]{:T(128)}, /*index=5*/bf16[2048,128]{1,0:T(8,...) while((s32[]{:T(128)}, f32[128,6,128]{2,0,1:T(8,128)S(1)}, ...), condition=%wide.region_21.22_spmd.clone, body=%wide.region_16.21_spmd.clone.sunk | while | flops 506528256 | bytes 13381159 | solution.py:168
  50.2 2.1 %conditional.7 = (f32[128,6,128]{2,0,1:T(8,128)S(1)}, f32[512,256]{0,1:T(8,128)S(1)}) conditional(s32[]{:T(128)} %clamp.19, f32[128,6,128]{2,0,1:T(8,128)S(1)} %get-tuple-element.1421, (f32[128,6,128]{2,0,1:T(8,128)S(1)}, s32[]{:T(128)}, s32[]{:T(128)}, bf16[128,6,128]{0,2,1:T(8,128)(2,1)S(1)}, ...), branch_computations={%region_17.17_spmd, %region_18.18_spmd, %region_19.19_spmd, %regio... | conditional | flops 506528256 | bytes 10758676 | solution.py:61
  50.2 0.1 broadcast_compare_fusion.5
  50.4 0.5 exponential_select_fusion.3
  50.9 0.3 convolution_bitcast_fusion.4
  51.2 0.4 multiply_convert_fusion
  51.6 0.3 fusion.56
  51.9 0.4 fusion.55
  52.3 0.2 copy.91
  52.5 0.8 constant_dynamic-update-slice_fusion.2
  53.4 2.1 %conditional.7 = (f32[128,6,128]{2,0,1:T(8,128)S(1)}, f32[512,256]{0,1:T(8,128)S(1)}) conditional(s32[]{:T(128)} %clamp.19, f32[128,6,128]{2,0,1:T(8,128)S(1)} %get-tuple-element.1421, (f32[128,6,128]{2,0,1:T(8,128)S(1)}, s32[]{:T(128)}, s32[]{:T(128)}, bf16[128,6,128]{0,2,1:T(8,128)(2,1)S(1)}, ...), branch_computations={%region_17.17_spmd, %region_18.18_spmd, %region_19.19_spmd, %regio... | conditional | flops 506528256 | bytes 10758676 | solution.py:61
  53.4 0.1 broadcast_compare_fusion.5
  53.5 0.5 exponential_select_fusion.3
  54.1 0.3 convolution_bitcast_fusion.4
  54.3 0.4 multiply_convert_fusion
  54.8 0.3 fusion.56
  55.0 0.4 fusion.55
  55.5 0.2 copy.91
  55.7 0.9 constant_dynamic-update-slice_fusion.2
  56.6 0.1 conditional.7
  56.6 0.1 broadcast.400
  56.7 0.2 copy.91
  56.9 0.9 constant_dynamic-update-slice_fusion.2
  57.7 0.1 conditional.7
  57.8 0.1 broadcast.400
  57.8 0.2 copy.91
  58.1 0.9 constant_dynamic-update-slice_fusion.2
  58.9 0.0 copy-start
  58.9 2.9 %copy.78 = f32[16,128,256]{1,2,0:T(8,128)} copy(f32[16,128,256]{2,1,0:T(8,128)} %bitcast.88) | data formatting | bytes 4194304 | tf_op jit(solution)/shard_map/reshape | solution.py:176
  61.8 0.0 copy-done
  61.8 13.2 %all-to-all-start = ((f32[16,128,256]{1,2,0:T(8,128)}), f32[16,128,256]{1,2,0:T(8,128)S(1)}, u32[]{:S(2)}, u32[]{:S(2)}) async-start(f32[16,128,256]{1,2,0:T(8,128)} %copy.78), calls=%async_computation | async-start | bytes 4194304 | tf_op jit(solution)/shard_map/all_to_all | solution.py:175
  75.0 0.2 copy.76
  75.2 0.9 copy.80
  76.1 46.3 %all-to-all-done = f32[16,128,256]{1,2,0:T(8,128)S(1)} async-done(((f32[16,128,256]{1,2,0:T(8,128)}), f32[16,128,256]{1,2,0:T(8,128)S(1)}, u32[]{:S(2)}, u32[]{:S(2)}) %all-to-all-start) | async-done | bytes 2097184 | tf_op jit(solution)/shard_map/all_to_all | solution.py:175
  122.4 0.1 reduce_sum.73
  122.5 0.7 copy.82
  123.2 0.7 copy.81
  (45 shorter events, 0.5 us)
Async XLA Ops:
  0.6 4.1 %copy-start.1 = (bf16[128,128]{1,0:T(8,128)(2,1)S(1)}, bf16[128,128]{1,0:T(8,128)(2,1)}, u32[]{:S(2)}) copy-start(bf16[128,128]{1,0:T(8,128)(2,1)} %param.52) | copy-start | bytes 98308
  0.6 21.2 %copy-start.2 = (bf16[128,128]{1,0:T(8,128)(2,1)S(1)}, bf16[128,128]{1,0:T(8,128)(2,1)}, u32[]{:S(2)}) copy-start(bf16[128,128]{1,0:T(8,128)(2,1)} %param.53) | copy-start | bytes 98308
  58.9 2.9 %copy-start = (f32[128,6]{0,1:T(8,128)}, f32[128,6]{0,1:T(8,128)S(1)}, u32[]{:S(2)}) copy-start(f32[128,6]{0,1:T(8,128)S(1)} %get-tuple-element.1469) | copy-start | bytes 9220
  61.8 60.6 %all-to-all-start = ((f32[16,128,256]{1,2,0:T(8,128)}), f32[16,128,256]{1,2,0:T(8,128)S(1)}, u32[]{:S(2)}, u32[]{:S(2)}) async-start(f32[16,128,256]{1,2,0:T(8,128)} %copy.78), calls=%async_computation | async-start | bytes 4194304 | tf_op jit(solution)/shard_map/all_to_all | solution.py:175
where the time goes:
time: 124 us
  waiting for transfers between devices  46.3 us (37%)
  blocking collectives  39.9 us (32%)
  starting transfers between devices  13.2 us (11%)
  local copies, waits for them, and re-layouts  13.1 us (11%)
  matrix products  5.79 us (5%)
  other arithmetic  4.14 us (3%)
    all_to_all x1, waiting for transfers between devices, body(): lax.all_to_all(partial_sums.reshape(ctx_count, tok_rows, 2 * head_dim), '...  46.3 us
    all_gather x1, blocking collectives, body(): value_piece = lax.all_gather(value_rows, 'ctx', axis=0, tiled=True)  22.8 us
    all_gather x1, blocking collectives, body(): key_piece = lax.all_gather(key_rows, 'ctx', axis=0, tiled=True)  17.1 us
    all_to_all x1, starting transfers between devices, body(): lax.all_to_all(partial_sums.reshape(ctx_count, tok_rows, 2 * head_dim), '...  13.2 us
    dynamic_update_slice x8, local copies, waits for them, and re-layouts, backward_step(): lax.dynamic_update_slice_in_dim(partial_sums, block_sums, key_start, 0)  4.17 us
    unnamed x12, local copies, waits for them, and re-layouts  3.83 us
    reshape x1, local copies, waits for them, and re-layouts, body(): partial_sums.reshape(ctx_count, tok_rows, 2 * head_dim)  2.89 us
  transfers between devices with their start and end apart: 1, of which 1 were waited for; matrix products, arithmetic and copies ran while one was open for 1% of the time, Pallas kernels for 0%

commit v1 on v0

--- a/solution.py
+++ b/solution.py
@@ -93,7 +93,22 @@
     row_peak = jnp.full((tok_rows, head_count), -1e30, jnp.float32)
     row_total = jnp.zeros((tok_rows, head_count), jnp.float32)
     weighted = jnp.zeros((tok_rows, head_count), jnp.float32)
-    key_piece = lax.all_gather(key_rows, "ctx", axis=0, tiled=True)
+    ways, here, step = (lax.axis_size("ctx"), lax.axis_index("ctx"), key_rows.shape[0])
+    shape = [n * ways if d == 0 else n for d, n in enumerate(key_rows.shape)]
+    key_piece = lax.dynamic_update_slice_in_dim(
+        jnp.zeros(shape, key_rows.dtype), key_rows, here * step, axis=0
+    )
+    going_up = going_down = key_rows
+    for far in range(1, ways // 2 + 1):
+        going_up = lax.ppermute(going_up, "ctx", [(d, (d + 1) % ways) for d in range(ways)])
+        key_piece = lax.dynamic_update_slice_in_dim(
+            key_piece, going_up, (here - far) % ways * step, axis=0
+        )
+        if 2 * far < ways:
+            going_down = lax.ppermute(going_down, "ctx", [(d, (d - 1) % ways) for d in range(ways)])
+            key_piece = lax.dynamic_update_slice_in_dim(
+                key_piece, going_down, (here + far) % ways * step, axis=0
+            )
     value_piece = lax.all_gather(value_rows, "ctx", axis=0, tiled=True)
     piece_rows = key_piece.shape[0]
     block_rows = math.gcd(piece_rows, 512)

time: 124 us -> 147 us (1.19)
  starting transfers between devices: 13.2 us -> 47.8 us
  blocking collectives: 39.9 us -> 18.4 us
  waiting for transfers between devices: 46.3 us -> 56 us
    ppermute x0 -> x15, starting transfers between devices: none -> 22.1 us  [the longest x8 21.2 us: body(): lax.ppermute(going_up, 'ctx', [(d, (d + 1) % ways) for d in range(ways)])]
    all_gather x1 -> x0, blocking collectives: 17.1 us -> none  [body(): key_piece = lax.all_gather(key_rows, 'ctx', axis=0, tiled=True)]
    all_to_all x1, starting transfers between devices: 13.2 us -> 25.6 us  [body(): lax.all_to_all(partial_sums.reshape(ctx_count, tok_rows, 2 * head_dim), '...]
    ppermute x0 -> x15, waiting for transfers between devices: none -> 9.67 us  [the longest x7 7.66 us: body(): lax.ppermute(going_down, 'ctx', [(d, (d - 1) % ways) for d in range(ways)])]
    all_gather x1, blocking collectives: 22.8 us -> 18.4 us  [body(): value_piece = lax.all_gather(value_rows, 'ctx', axis=0, tiled=True)]
    unnamed x12 -> x10, local copies, waits for them, and re-layouts: 3.83 us -> 2.89 us
  transfers between devices with their start and end apart: 1 -> 16, of which waited for: 1 -> 8; matrix products, arithmetic and copies ran while one was open for 1% -> 4% of each run, Pallas kernels for 0% -> 0%
where the time goes in v1:
time: 147 us
  waiting for transfers between devices  56 us (38%)
  starting transfers between devices  47.8 us (33%)
  blocking collectives  18.4 us (13%)
  local copies, waits for them, and re-layouts  13.1 us (9%)
  matrix products  5.79 us (4%)
  other arithmetic  4.13 us (3%)
    all_to_all x1, waiting for transfers between devices, body(): lax.all_to_all(partial_sums.reshape(ctx_count, tok_rows, 2 * head_dim), '...  46.3 us
    all_to_all x1, starting transfers between devices, body(): lax.all_to_all(partial_sums.reshape(ctx_count, tok_rows, 2 * head_dim), '...  25.6 us
    ppermute x8, starting transfers between devices, body(): lax.ppermute(going_up, 'ctx', [(d, (d + 1) % ways) for d in range(ways)])  21.2 us
    all_gather x1, blocking collectives, body(): value_piece = lax.all_gather(value_rows, 'ctx', axis=0, tiled=True)  18.4 us
    ppermute x7, waiting for transfers between devices, body(): lax.ppermute(going_down, 'ctx', [(d, (d - 1) % ways) for d in range(ways)])  7.66 us
    dynamic_update_slice x8, local copies, waits for them, and re-layouts, backward_step(): lax.dynamic_update_slice_in_dim(partial_sums, block_sums, key_start, 0)  4.15 us
  transfers between devices with their start and end apart: 16, of which 8 were waited for; matrix products, arithmetic and copies ran while one was open for 4% of the time, Pallas kernels for 0%

profile of v1, /device:TPU:13, one launch (start us, length us, event | category | flops | bytes accessed | tf_op | source)
XLA Modules:
  0.0 147.1 jit_solution(10030525620119498611)
XLA Ops:
  0.6 0.7 collective-permute-start.1
  1.4 2.0 %collective-permute-start = (bf16[128,128]{1,0:T(8,128)(2,1)}, bf16[128,128]{1,0:T(8,128)(2,1)S(1)}, u32[]{:S(2)}, u32[]{:S(2)}) collective-permute-start(bf16[128,128]{1,0:T(8,128)(2,1)} %param.52), channel_id=1, source_target_pairs={{0,2},{2,4},{4,6},{6,8},{8,10},{10,12},{12,14},{14,16},{16,18},{18... | collective-permute-start | bytes 98312 | tf_op jit(solution)/shard_map/ppermute | solution.py:103
  3.3 18.4 %all_gather.3 = bf16[2048,128]{1,0:T(8,128)(2,1)S(1)} all-gather(bf16[128,128]{1,0:T(8,128)(2,1)} %param.53), channel_id=1, replica_groups=mesh['ctx'=16,'head'=2] {'ctx'}, dimensions={0}, use_global_device_ids=true | all-gather | bytes 557056 | tf_op jit(solution)/shard_map/all_gather | solution.py:112
  21.8 0.7 fusion.61
  22.4 0.7 select_reduce_fusion.3
  23.2 1.0 multiply_convert_fusion.1
  24.3 0.8 constant_dynamic-update-slice_fusion.16
  25.3 0.2 copy.73
  25.5 0.2 copy.75
  25.7 0.2 copy.72
  25.9 0.2 copy.74
  26.1 0.2 collective-permute-start.3
  26.4 2.5 %collective-permute-start.2 = (bf16[128,128]{1,0:T(8,128)(2,1)S(1)}, bf16[128,128]{1,0:T(8,128)(2,1)S(1)}, u32[]{:S(2)}, u32[]{:S(2)}) collective-permute-start(bf16[128,128]{1,0:T(8,128)(2,1)S(1)} %collective-permute-done), channel_id=1, source_target_pairs={{0,2},{2,4},{4,6},{6,8},{8,10},{10,12},{12,14},{14,16},{16,18},{18... | collective-permute-start | bytes 98312 | tf_op jit(solution)/shard_map/ppermute | solution.py:103
  28.9 1.6 %collective-permute-done.3 = bf16[128,128]{1,0:T(8,128)(2,1)S(1)} collective-permute-done((bf16[128,128]{1,0:T(8,128)(2,1)S(1)}, bf16[128,128]{1,0:T(8,128)(2,1)S(1)}, u32[]{:S(2)}, u32[]{:S(2)}) %collective-permute-start.3) | collective-permute-done | bytes 32800 | tf_op jit(solution)/shard_map/ppermute | solution.py:108
  30.5 2.7 %collective-permute-start.4 = (bf16[128,128]{1,0:T(8,128)(2,1)S(1)}, bf16[128,128]{1,0:T(8,128)(2,1)S(1)}, u32[]{:S(2)}, u32[]{:S(2)}) collective-permute-start(bf16[128,128]{1,0:T(8,128)(2,1)S(1)} %collective-permute-done.2), channel_id=1, source_target_pairs={{0,2},{2,4},{4,6},{6,8},{8,10},{10,12},{12,14},{14,16},{16,18},{18... | collective-permute-start | bytes 98312 | tf_op jit(solution)/shard_map/ppermute | solution.py:103
  33.2 1.5 %collective-permute-done.5 = bf16[128,128]{1,0:T(8,128)(2,1)S(1)} collective-permute-done((bf16[128,128]{1,0:T(8,128)(2,1)S(1)}, bf16[128,128]{1,0:T(8,128)(2,1)S(1)}, u32[]{:S(2)}, u32[]{:S(2)}) %collective-permute-start.5) | collective-permute-done | bytes 32800 | tf_op jit(solution)/shard_map/ppermute | solution.py:108
  34.7 2.7 %collective-permute-start.6 = (bf16[128,128]{1,0:T(8,128)(2,1)S(1)}, bf16[128,128]{1,0:T(8,128)(2,1)S(1)}, u32[]{:S(2)}, u32[]{:S(2)}) collective-permute-start(bf16[128,128]{1,0:T(8,128)(2,1)S(1)} %collective-permute-done.4), channel_id=1, source_target_pairs={{0,2},{2,4},{4,6},{6,8},{8,10},{10,12},{12,14},{14,16},{16,18},{18... | collective-permute-start | bytes 98312 | tf_op jit(solution)/shard_map/ppermute | solution.py:103
  37.4 1.5 %collective-permute-done.7 = bf16[128,128]{1,0:T(8,128)(2,1)S(1)} collective-permute-done((bf16[128,128]{1,0:T(8,128)(2,1)S(1)}, bf16[128,128]{1,0:T(8,128)(2,1)S(1)}, u32[]{:S(2)}, u32[]{:S(2)}) %collective-permute-start.7) | collective-permute-done | bytes 32800 | tf_op jit(solution)/shard_map/ppermute | solution.py:108
  39.0 2.7 %collective-permute-start.8 = (bf16[128,128]{1,0:T(8,128)(2,1)S(1)}, bf16[128,128]{1,0:T(8,128)(2,1)S(1)}, u32[]{:S(2)}, u32[]{:S(2)}) collective-permute-start(bf16[128,128]{1,0:T(8,128)(2,1)S(1)} %collective-permute-done.6), channel_id=1, source_target_pairs={{0,2},{2,4},{4,6},{6,8},{8,10},{10,12},{12,14},{14,16},{16,18},{18... | collective-permute-start | bytes 98312 | tf_op jit(solution)/shard_map/ppermute | solution.py:103
  41.7 1.5 %collective-permute-done.9 = bf16[128,128]{1,0:T(8,128)(2,1)S(1)} collective-permute-done((bf16[128,128]{1,0:T(8,128)(2,1)S(1)}, bf16[128,128]{1,0:T(8,128)(2,1)S(1)}, u32[]{:S(2)}, u32[]{:S(2)}) %collective-permute-start.9) | collective-permute-done | bytes 32800 | tf_op jit(solution)/shard_map/ppermute | solution.py:108
  43.2 2.7 %collective-permute-start.10 = (bf16[128,128]{1,0:T(8,128)(2,1)S(1)}, bf16[128,128]{1,0:T(8,128)(2,1)S(1)}, u32[]{:S(2)}, u32[]{:S(2)}) collective-permute-start(bf16[128,128]{1,0:T(8,128)(2,1)S(1)} %collective-permute-done.8), channel_id=1, source_target_pairs={{0,2},{2,4},{4,6},{6,8},{8,10},{10,12},{12,14},{14,16},{16,18},{18... | collective-permute-start | bytes 98312 | tf_op jit(solution)/shard_map/ppermute | solution.py:103
  45.9 1.5 %collective-permute-done.11 = bf16[128,128]{1,0:T(8,128)(2,1)S(1)} collective-permute-done((bf16[128,128]{1,0:T(8,128)(2,1)S(1)}, bf16[128,128]{1,0:T(8,128)(2,1)S(1)}, u32[]{:S(2)}, u32[]{:S(2)}) %collective-permute-start.11) | collective-permute-done | bytes 32800 | tf_op jit(solution)/shard_map/ppermute | solution.py:108
  47.4 2.7 %collective-permute-start.12 = (bf16[128,128]{1,0:T(8,128)(2,1)S(1)}, bf16[128,128]{1,0:T(8,128)(2,1)S(1)}, u32[]{:S(2)}, u32[]{:S(2)}) collective-permute-start(bf16[128,128]{1,0:T(8,128)(2,1)S(1)} %collective-permute-done.10), channel_id=1, source_target_pairs={{0,2},{2,4},{4,6},{6,8},{8,10},{10,12},{12,14},{14,16},{16,18},{18... | collective-permute-start | bytes 98312 | tf_op jit(solution)/shard_map/ppermute | solution.py:103
  50.2 1.0 collective-permute-done.12
  51.2 3.2 %collective-permute-start.14 = (bf16[128,128]{1,0:T(8,128)(2,1)S(1)}, bf16[128,128]{1,0:T(8,128)(2,1)S(1)}, u32[]{:S(2)}, u32[]{:S(2)}) collective-permute-start(bf16[128,128]{1,0:T(8,128)(2,1)S(1)} %collective-permute-done.12), channel_id=1, source_target_pairs={{0,2},{2,4},{4,6},{6,8},{8,10},{10,12},{12,14},{14,16},{16,18},{18... | collective-permute-start | bytes 98312 | tf_op jit(solution)/shard_map/ppermute | solution.py:103
  54.4 1.0 collective-permute-done.14
  55.4 3.9 %while.53 = (s32[]{:T(128)}, f32[128,6]{0,1:T(8,128)S(1)}, f32[128,6]{0,1:T(8,128)S(1)}, f32[128,6]{0,1:T(8,128)S(1)}, s32[]{:T(128)}, /*index=5*/s32[]{:T(128)}...) while((s32[]{:T(128)}, f32[128,6]{0,1:T(8,128)S(1)}, ...), condition=%wide.region_15.16_spmd.clone, body=%wide.region_1.15_spmd.clone.sunk | while | flops 205327120 | bytes 6221379 | solution.py:122
  55.5 1.7 %conditional.6 = ((f32[128,6]{0,1:T(8,128)S(1)}, f32[128,6]{0,1:T(8,128)S(1)}, f32[128,6]{0,1:T(8,128)S(1)})) conditional(s32[]{:T(128)} %clamp.18, (f32[128,6]{0,1:T(8,128)S(1)}, f32[128,6]{0,1:T(8,128)S(1)}, f32[128,6]{0,1:T(8,128)S(1)}) %tuple.202, (f32[128,6]{0,1:T(8,128)S(1)}, s32[]{:T(128)}, s32[]{:T(128)}, ...), branch_computations={%region_2.2_spmd, %region_3.6_spmd, %region_7.0_spmd, %region_11.0... | conditional | flops 205327104 | bytes 5696036 | solution.py:61
  55.7 0.5 select_reduce_fusion.2
  56.2 0.6 multiply_reduce_fusion
  56.7 0.5 fusion.20
  57.3 1.7 %conditional.6 = ((f32[128,6]{0,1:T(8,128)S(1)}, f32[128,6]{0,1:T(8,128)S(1)}, f32[128,6]{0,1:T(8,128)S(1)})) conditional(s32[]{:T(128)} %clamp.18, (f32[128,6]{0,1:T(8,128)S(1)}, f32[128,6]{0,1:T(8,128)S(1)}, f32[128,6]{0,1:T(8,128)S(1)}) %tuple.202, (f32[128,6]{0,1:T(8,128)S(1)}, s32[]{:T(128)}, s32[]{:T(128)}, ...), branch_computations={%region_2.2_spmd, %region_3.6_spmd, %region_7.0_spmd, %region_11.0... | conditional | flops 205327104 | bytes 5696036 | solution.py:61
  57.5 0.5 select_reduce_fusion.2
  58.0 0.6 multiply_reduce_fusion
  58.5 0.5 fusion.20
  59.4 1.5 %broadcast_in_dim.128.clone = f32[2048,256]{1,0:T(8,128)} broadcast(f32[]{:T(128)} %constant.571.clone.1), dimensions={} | broadcast | bytes 2097156 | tf_op jit(solution)/shard_map/broadcast_in_dim | solution.py:187
  60.9 8.7 %while.54 = (s32[]{:T(128)}, f32[128,6,128]{2,0,1:T(8,128)S(1)}, f32[2048,256]{1,0:T(8,128)}, s32[]{:T(128)}, s32[]{:T(128)}, /*index=5*/bf16[2048,128]{1,0:T(8,...) while((s32[]{:T(128)}, f32[128,6,128]{2,0,1:T(8,128)S(1)}, ...), condition=%wide.region_21.22_spmd.clone, body=%wide.region_16.21_spmd.clone.sunk | while | flops 506528256 | bytes 13381159 | solution.py:183
  60.9 2.1 %conditional.7 = (f32[128,6,128]{2,0,1:T(8,128)S(1)}, f32[512,256]{0,1:T(8,128)S(1)}) conditional(s32[]{:T(128)} %clamp.19, f32[128,6,128]{2,0,1:T(8,128)S(1)} %get-tuple-element.1421, (f32[128,6,128]{2,0,1:T(8,128)S(1)}, s32[]{:T(128)}, s32[]{:T(128)}, bf16[128,6,128]{0,2,1:T(8,128)(2,1)S(1)}, ...), branch_computations={%region_17.17_spmd, %region_18.18_spmd, %region_19.19_spmd, %regio... | conditional | flops 506528256 | bytes 10758676 | solution.py:61
  61.1 0.5 exponential_select_fusion.3
  61.6 0.3 convolution_bitcast_fusion.4
  61.9 0.4 multiply_convert_fusion
  62.3 0.3 fusion.56
  62.6 0.4 fusion.55
  63.0 0.2 copy.91
  63.2 0.8 constant_dynamic-update-slice_fusion.18
  64.1 2.1 %conditional.7 = (f32[128,6,128]{2,0,1:T(8,128)S(1)}, f32[512,256]{0,1:T(8,128)S(1)}) conditional(s32[]{:T(128)} %clamp.19, f32[128,6,128]{2,0,1:T(8,128)S(1)} %get-tuple-element.1421, (f32[128,6,128]{2,0,1:T(8,128)S(1)}, s32[]{:T(128)}, s32[]{:T(128)}, bf16[128,6,128]{0,2,1:T(8,128)(2,1)S(1)}, ...), branch_computations={%region_17.17_spmd, %region_18.18_spmd, %region_19.19_spmd, %regio... | conditional | flops 506528256 | bytes 10758676 | solution.py:61
  64.2 0.5 exponential_select_fusion.3
  64.8 0.3 convolution_bitcast_fusion.4
  65.1 0.4 multiply_convert_fusion
  65.5 0.3 fusion.56
  65.7 0.4 fusion.55
  66.2 0.2 copy.91
  66.4 0.8 constant_dynamic-update-slice_fusion.18
  67.4 0.2 copy.91
  67.6 0.8 constant_dynamic-update-slice_fusion.18
  68.5 0.2 copy.91
  68.8 0.8 constant_dynamic-update-slice_fusion.18
  69.6 2.9 %copy.78 = f32[16,128,256]{1,2,0:T(8,128)} copy(f32[16,128,256]{2,1,0:T(8,128)} %bitcast.88) | data formatting | bytes 4194304 | tf_op jit(solution)/shard_map/reshape | solution.py:191
  72.5 25.6 %all-to-all-start = ((f32[16,128,256]{1,2,0:T(8,128)}), f32[16,128,256]{1,2,0:T(8,128)S(1)}, u32[]{:S(2)}, u32[]{:S(2)}) async-start(f32[16,128,256]{1,2,0:T(8,128)} %copy.78), calls=%async_computation | async-start | bytes 4194304 | tf_op jit(solution)/shard_map/all_to_all | solution.py:190
  98.1 0.2 copy.76
  98.3 0.9 copy.80
  99.2 46.3 %all-to-all-done = f32[16,128,256]{1,2,0:T(8,128)S(1)} async-done(((f32[16,128,256]{1,2,0:T(8,128)}), f32[16,128,256]{1,2,0:T(8,128)S(1)}, u32[]{:S(2)}, u32[]{:S(2)}) %all-to-all-start) | async-done | bytes 2097184 | tf_op jit(solution)/shard_map/all_to_all | solution.py:190
  145.6 0.7 copy.82
  146.4 0.7 copy.81
  (88 shorter events, 1.6 us)
Async XLA Ops:
  0.6 25.1 %copy-start = (bf16[128,768]{1,0:T(8,128)(2,1)S(1)}, bf16[128,768]{1,0:T(8,128)(2,1)}, u32[]{:S(2)}) copy-start(bf16[128,768]{1,0:T(8,128)(2,1)} %param.51) | copy-start | bytes 589828
  0.6 25.5 %collective-permute-start.1 = (bf16[128,128]{1,0:T(8,128)(2,1)}, bf16[128,128]{1,0:T(8,128)(2,1)S(1)}, u32[]{:S(2)}, u32[]{:S(2)}) collective-permute-start(bf16[128,128]{1,0:T(8,128)(2,1)} %param.52), channel_id=1, source_target_pairs={{0,30},{2,0},{4,2},{6,4},{8,6},{10,8},{12,10},{14,12},{16,14},{18,... | collective-permute-start | bytes 98312 | tf_op jit(solution)/shard_map/ppermute | solution.py:108
  1.4 25.0 %collective-permute-start = (bf16[128,128]{1,0:T(8,128)(2,1)}, bf16[128,128]{1,0:T(8,128)(2,1)S(1)}, u32[]{:S(2)}, u32[]{:S(2)}) collective-permute-start(bf16[128,128]{1,0:T(8,128)(2,1)} %param.52), channel_id=1, source_target_pairs={{0,2},{2,4},{4,6},{6,8},{8,10},{10,12},{12,14},{14,16},{16,18},{18... | collective-permute-start | bytes 98312 | tf_op jit(solution)/shard_map/ppermute | solution.py:103
  26.1 4.3 %collective-permute-start.3 = (bf16[128,128]{1,0:T(8,128)(2,1)S(1)}, bf16[128,128]{1,0:T(8,128)(2,1)S(1)}, u32[]{:S(2)}, u32[]{:S(2)}) collective-permute-start(bf16[128,128]{1,0:T(8,128)(2,1)S(1)} %collective-permute-done.1), channel_id=1, source_target_pairs={{0,30},{2,0},{4,2},{6,4},{8,6},{10,8},{12,10},{14,12},{16,14},{18,... | collective-permute-start | bytes 98312 | tf_op jit(solution)/shard_map/ppermute | solution.py:108
  26.4 4.1 %collective-permute-start.2 = (bf16[128,128]{1,0:T(8,128)(2,1)S(1)}, bf16[128,128]{1,0:T(8,128)(2,1)S(1)}, u32[]{:S(2)}, u32[]{:S(2)}) collective-permute-start(bf16[128,128]{1,0:T(8,128)(2,1)S(1)} %collective-permute-done), channel_id=1, source_target_pairs={{0,2},{2,4},{4,6},{6,8},{8,10},{10,12},{12,14},{14,16},{16,18},{18... | collective-permute-start | bytes 98312 | tf_op jit(solution)/shard_map/ppermute | solution.py:103
  30.5 4.2 %collective-permute-start.5 = (bf16[128,128]{1,0:T(8,128)(2,1)S(1)}, bf16[128,128]{1,0:T(8,128)(2,1)S(1)}, u32[]{:S(2)}, u32[]{:S(2)}) collective-permute-start(bf16[128,128]{1,0:T(8,128)(2,1)S(1)} %collective-permute-done.3), channel_id=1, source_target_pairs={{0,30},{2,0},{4,2},{6,4},{8,6},{10,8},{12,10},{14,12},{16,14},{18,... | collective-permute-start | bytes 98312 | tf_op jit(solution)/shard_map/ppermute | solution.py:108
  30.5 4.2 %collective-permute-start.4 = (bf16[128,128]{1,0:T(8,128)(2,1)S(1)}, bf16[128,128]{1,0:T(8,128)(2,1)S(1)}, u32[]{:S(2)}, u32[]{:S(2)}) collective-permute-start(bf16[128,128]{1,0:T(8,128)(2,1)S(1)} %collective-permute-done.2), channel_id=1, source_target_pairs={{0,2},{2,4},{4,6},{6,8},{8,10},{10,12},{12,14},{14,16},{16,18},{18... | collective-permute-start | bytes 98312 | tf_op jit(solution)/shard_map/ppermute | solution.py:103
  34.7 4.2 %collective-permute-start.7 = (bf16[128,128]{1,0:T(8,128)(2,1)S(1)}, bf16[128,128]{1,0:T(8,128)(2,1)S(1)}, u32[]{:S(2)}, u32[]{:S(2)}) collective-permute-start(bf16[128,128]{1,0:T(8,128)(2,1)S(1)} %collective-permute-done.5), channel_id=1, source_target_pairs={{0,30},{2,0},{4,2},{6,4},{8,6},{10,8},{12,10},{14,12},{16,14},{18,... | collective-permute-start | bytes 98312 | tf_op jit(solution)/shard_map/ppermute | solution.py:108
  34.7 4.2 %collective-permute-start.6 = (bf16[128,128]{1,0:T(8,128)(2,1)S(1)}, bf16[128,128]{1,0:T(8,128)(2,1)S(1)}, u32[]{:S(2)}, u32[]{:S(2)}) collective-permute-start(bf16[128,128]{1,0:T(8,128)(2,1)S(1)} %collective-permute-done.4), channel_id=1, source_target_pairs={{0,2},{2,4},{4,6},{6,8},{8,10},{10,12},{12,14},{14,16},{16,18},{18... | collective-permute-start | bytes 98312 | tf_op jit(solution)/shard_map/ppermute | solution.py:103
  39.0 4.2 %collective-permute-start.9 = (bf16[128,128]{1,0:T(8,128)(2,1)S(1)}, bf16[128,128]{1,0:T(8,128)(2,1)S(1)}, u32[]{:S(2)}, u32[]{:S(2)}) collective-permute-start(bf16[128,128]{1,0:T(8,128)(2,1)S(1)} %collective-permute-done.7), channel_id=1, source_target_pairs={{0,30},{2,0},{4,2},{6,4},{8,6},{10,8},{12,10},{14,12},{16,14},{18,... | collective-permute-start | bytes 98312 | tf_op jit(solution)/shard_map/ppermute | solution.py:108
  39.0 4.2 %collective-permute-start.8 = (bf16[128,128]{1,0:T(8,128)(2,1)S(1)}, bf16[128,128]{1,0:T(8,128)(2,1)S(1)}, u32[]{:S(2)}, u32[]{:S(2)}) collective-permute-start(bf16[128,128]{1,0:T(8,128)(2,1)S(1)} %collective-permute-done.6), channel_id=1, source_target_pairs={{0,2},{2,4},{4,6},{6,8},{8,10},{10,12},{12,14},{14,16},{16,18},{18... | collective-permute-start | bytes 98312 | tf_op jit(solution)/shard_map/ppermute | solution.py:103
  43.2 4.2 %collective-permute-start.11 = (bf16[128,128]{1,0:T(8,128)(2,1)S(1)}, bf16[128,128]{1,0:T(8,128)(2,1)S(1)}, u32[]{:S(2)}, u32[]{:S(2)}) collective-permute-start(bf16[128,128]{1,0:T(8,128)(2,1)S(1)} %collective-permute-done.9), channel_id=1, source_target_pairs={{0,30},{2,0},{4,2},{6,4},{8,6},{10,8},{12,10},{14,12},{16,14},{18,... | collective-permute-start | bytes 98312 | tf_op jit(solution)/shard_map/ppermute | solution.py:108
  43.2 4.2 %collective-permute-start.10 = (bf16[128,128]{1,0:T(8,128)(2,1)S(1)}, bf16[128,128]{1,0:T(8,128)(2,1)S(1)}, u32[]{:S(2)}, u32[]{:S(2)}) collective-permute-start(bf16[128,128]{1,0:T(8,128)(2,1)S(1)} %collective-permute-done.8), channel_id=1, source_target_pairs={{0,2},{2,4},{4,6},{6,8},{8,10},{10,12},{12,14},{14,16},{16,18},{18... | collective-permute-start | bytes 98312 | tf_op jit(solution)/shard_map/ppermute | solution.py:103
  47.4 7.0 %collective-permute-start.13 = (bf16[128,128]{1,0:T(8,128)(2,1)S(1)}, bf16[128,128]{1,0:T(8,128)(2,1)S(1)}, u32[]{:S(2)}, u32[]{:S(2)}) collective-permute-start(bf16[128,128]{1,0:T(8,128)(2,1)S(1)} %collective-permute-done.11), channel_id=1, source_target_pairs={{0,30},{2,0},{4,2},{6,4},{8,6},{10,8},{12,10},{14,12},{16,14},{18,... | collective-permute-start | bytes 98312 | tf_op jit(solution)/shard_map/ppermute | solution.py:108
  47.4 3.7 %collective-permute-start.12 = (bf16[128,128]{1,0:T(8,128)(2,1)S(1)}, bf16[128,128]{1,0:T(8,128)(2,1)S(1)}, u32[]{:S(2)}, u32[]{:S(2)}) collective-permute-start(bf16[128,128]{1,0:T(8,128)(2,1)S(1)} %collective-permute-done.10), channel_id=1, source_target_pairs={{0,2},{2,4},{4,6},{6,8},{8,10},{10,12},{12,14},{14,16},{16,18},{18... | collective-permute-start | bytes 98312 | tf_op jit(solution)/shard_map/ppermute | solution.py:103
  51.2 4.2 %collective-permute-start.14 = (bf16[128,128]{1,0:T(8,128)(2,1)S(1)}, bf16[128,128]{1,0:T(8,128)(2,1)S(1)}, u32[]{:S(2)}, u32[]{:S(2)}) collective-permute-start(bf16[128,128]{1,0:T(8,128)(2,1)S(1)} %collective-permute-done.12), channel_id=1, source_target_pairs={{0,2},{2,4},{4,6},{6,8},{8,10},{10,12},{12,14},{14,16},{16,18},{18... | collective-permute-start | bytes 98312 | tf_op jit(solution)/shard_map/ppermute | solution.py:103
  69.6 2.9 %copy-start.1 = (f32[128,6]{0,1:T(8,128)}, f32[128,6]{0,1:T(8,128)S(1)}, u32[]{:S(2)}) copy-start(f32[128,6]{0,1:T(8,128)S(1)} %get-tuple-element.1469) | copy-start | bytes 9220
  72.5 73.0 %all-to-all-start = ((f32[16,128,256]{1,2,0:T(8,128)}), f32[16,128,256]{1,2,0:T(8,128)S(1)}, u32[]{:S(2)}, u32[]{:S(2)}) async-start(f32[16,128,256]{1,2,0:T(8,128)} %copy.78), calls=%async_computation | async-start | bytes 4194304 | tf_op jit(solution)/shard_map/all_to_all | solution.py:190
